TPU v7x, 256 devices: a whole 4x4x8 slice. The times are simulated.
256 devices in a mesh: req: 64 (over y, z_lo, x, core), tp: 4 (over z_hi).
Axes of the slice: x: 4, y: 4, z: 8 (z_hi: 4, z_lo: 2; z = z_hi * 2 + z_lo), core: 2. Of those that a mesh axis runs over, the one named last changes fastest.
Arguments:
- tokens: bfloat16 [16384, 2048], P('req'), may hold values from -6 to 6
- norm_gain: float32 [2048], replicated, may hold values from 0.25 to 1.75
- w_query: bfloat16 [2048, 2048], P(None, 'tp'), may hold values from -1 to 1
- w_key: bfloat16 [2048, 2048], P(None, 'tp'), may hold values from -1 to 1
- w_value: bfloat16 [2048, 2048], P(None, 'tp'), may hold values from -0.125 to 0.125
- w_out: bfloat16 [2048, 2048], P('tp'), may hold values from -0.125 to 0.125
- lambdas: float32 [4, 8, 128], P(None, 'tp'), may hold values from -1 to 1
- sub_gain: float32 [8, 256], P('tp'), may hold values from 0.5 to 2
- lengths: int32 [4], replicated, may hold values from 1 to 8192, 16384 in all
Outputs:
- hidden: bfloat16 [16384, 2048], P('req')
- key_cache: bfloat16 [16384, 2048], P('req', 'tp')
- value_cache: bfloat16 [16384, 2048], P('req', 'tp')
Inputs may be any that keep to these rules, and one draw needn't show every extreme that they name: The lengths sum to 16384; the longest is exactly 8192.
All inputs are finite; a program needn't handle non-finite values.
Results may differ from a plain program's by a relative error of at most 0.007.
Values may be sent and summed in bfloat16 or wider, within the bound.
No kernel may reach another device: no remote copies, remote signals or barrier semaphores. Data moves between devices by JAX's collectives and lax.ppermute only.
A program may use at most 128 MiB of HBM per device.

v0:
```python
import math
import jax
import jax.numpy as jnp
from jax import lax
from jax.sharding import PartitionSpec as P

QK = 128
VD = 256
lambda_start = 0.8 - 0.6 * math.exp(-3.3)
masked_score = -1e30


def shifted(value, axis, steps):
    count = lax.axis_size(axis)
    first, last = (max(0, -steps), min(count, count - steps))
    return lax.ppermute(value, axis, [(source, source + steps) for source in range(first, last)])


def locate(index, lengths):
    ends = jnp.cumsum(lengths)
    starts = ends - lengths
    segment = jnp.sum((ends[None, :] <= index[:, None]).astype(jnp.int32), axis=1)
    hit = jnp.arange(lengths.shape[0], dtype=jnp.int32)[None, :] == segment[:, None]
    begin = jnp.sum(jnp.where(hit, starts[None, :], 0), axis=1)
    return (segment, index - begin)


def rotate(proj, position):
    half = proj.shape[-1] // 2
    freq = 10000.0 ** (-jnp.arange(half, dtype=jnp.float32) / half)
    angle = position.astype(jnp.float32)[:, None] * freq[None, :]
    cosine = jnp.cos(angle)[:, None, None, :]
    sine = jnp.sin(angle)[:, None, None, :]
    front = proj[..., :half]
    back = proj[..., half:]
    return jnp.concatenate([front * cosine - back * sine, back * cosine + front * sine], axis=-1)


def on_device(tokens, norm_gain, w_query, w_key, w_value, w_out, lambdas, sub_gain, lengths):
    rows = tokens.shape[0]
    heads = w_query.shape[1] // (2 * QK)
    key_cols = heads * 2 * QK
    total = rows * lax.axis_size("req")
    longest = min(8192, total // 2)
    reach = longest // rows
    first = lax.axis_index("req") * rows
    local_index = first + jnp.arange(rows, dtype=jnp.int32)
    seg_query, pos_query = locate(local_index, lengths)
    xf = tokens.astype(jnp.float32)
    normed = (xf * lax.rsqrt(jnp.mean(xf * xf, axis=-1, keepdims=True) + 1e-06) * norm_gain).astype(
        jnp.bfloat16
    )
    query = rotate(
        jnp.dot(normed, w_query, preferred_element_type=jnp.float32).reshape(rows, heads, 2, QK),
        pos_query,
    ).astype(jnp.bfloat16)
    keys = rotate(
        jnp.dot(normed, w_key, preferred_element_type=jnp.float32).reshape(rows, heads, 2, QK),
        pos_query,
    ).astype(jnp.bfloat16)
    values = jnp.dot(normed, w_value, preferred_element_type=jnp.float32).astype(jnp.bfloat16)
    key_flat = keys.reshape(rows, key_cols)
    own = jnp.concatenate([key_flat, values], axis=1)
    lam = (
        jnp.exp(jnp.sum(lambdas[0] * lambdas[1], axis=-1))
        - jnp.exp(jnp.sum(lambdas[2] * lambdas[3], axis=-1))
        + lambda_start
    )
    scale = QK ** (-0.5)

    def absorb(state, shard, anchor):
        key_index = anchor + jnp.arange(rows, dtype=jnp.int32)
        key_seg, unused = locate(key_index, lengths)
        allowed = (
            (key_index >= 0)[None, :]
            & (key_index[None, :] <= local_index[:, None])
            & (key_seg[None, :] == seg_query[:, None])
        )

        def compute(carry):
            top, mass, acc = carry
            shard_keys = shard[:, :key_cols].reshape(rows, heads, 2, QK)
            shard_values = shard[:, key_cols:].reshape(rows, heads, VD)
            scores = (
                jnp.einsum("qhmd,khmd->mhqk", query, shard_keys, preferred_element_type=jnp.float32)
                * scale
            )
            scores = jnp.where(allowed, scores, masked_score)
            new_top = jnp.maximum(top, jnp.max(scores, axis=-1))
            weights = jnp.where(allowed, jnp.exp(scores - new_top[..., None]), 0.0)
            fade = jnp.exp(top - new_top)
            mass = mass * fade + jnp.sum(weights, axis=-1)
            acc = acc * fade[..., None] + jnp.einsum(
                "mhqk,khv->mhqv",
                weights.astype(jnp.bfloat16),
                shard_values,
                preferred_element_type=jnp.float32,
            )
            return (new_top, mass, acc)

        def keep(carry):
            return carry

        return lax.cond(jnp.any(allowed), compute, keep, state)

    start = (
        jnp.full((2, heads, rows), masked_score, jnp.float32),
        jnp.zeros((2, heads, rows), jnp.float32),
        jnp.zeros((2, heads, rows, VD), jnp.float32),
    )
    arriving = shifted(own, "req", 1)
    state = absorb(start, own, first)

    def turn(step, carry):
        current, moving = carry
        following = shifted(moving, "req", 1)
        return (absorb(current, moving, first - (step + 1) * rows), following)

    state, moving = lax.fori_loop(0, reach - 1, turn, (state, arriving))
    state = absorb(state, moving, first - reach * rows)
    top, mass, acc = state
    attended = acc / mass[..., None]
    diff = attended[0] - lam[:, None, None] * attended[1]
    normed_heads = (
        diff
        * lax.rsqrt(jnp.mean(diff * diff, axis=-1, keepdims=True) + 1e-05)
        * sub_gain[:, None, :]
        * (1.0 - lambda_start)
    )
    merged = jnp.transpose(normed_heads, (1, 0, 2)).reshape(rows, heads * VD).astype(jnp.bfloat16)
    summed = lax.psum(
        jnp.dot(merged, w_out, preferred_element_type=jnp.float32).astype(jnp.bfloat16), "tp"
    ).astype(jnp.float32)
    hidden = (xf + summed).astype(jnp.bfloat16)
    return (hidden, key_flat, values)


def solution(mesh):
    in_specs = (
        P("req", None),
        P(),
        P(None, "tp"),
        P(None, "tp"),
        P(None, "tp"),
        P("tp", None),
        P(None, "tp", None),
        P("tp", None),
        P(),
    )
    out_specs = (P("req", None), P("req", "tp"), P("req", "tp"))
    return jax.shard_map(
        on_device, mesh=mesh, in_specs=in_specs, out_specs=out_specs, check_vma=False
    )
```

profile of v0, /device:TPU:1, one launch (start us, length us, event | category | flops | bytes accessed | tf_op | source)
XLA Modules:
  0.0 609.4 jit_solution(146816331163059637)
XLA Ops:
  21.9 4.5 collective-permute-start.1
  32.9 7.5 %conditional.3 = (f32[2,2,256]{2,1,0:T(2,128)}, f32[2,2,256]{2,1,0:T(2,128)S(1)}, f32[2,2,256,256]{3,2,0,1:T(8,128)S(1)}) conditional(s32[]{:T(128)} %convert_element_type.87, () %tuple.51, (pred[256,256]{0,1:T(8,128)(4,1)S(1)}, bf16[256,2,2,128]{3,0,1,2:T(8,128)(2,1)S(1)}, bf16[256,2,2,128]{3,0,1,2:T(8,128)(2,1)}, bf16[256,512]{1,0:T(8,128)(2,1)}) %tuple.125), branch_computations={%region_7.8_spmd, %region_8.11_spmd} | conditional | flops 203427840 | bytes 5685272 | solution.py:104
  42.7 417.4 %while.23 = (s32[]{:T(128)}, f32[2,2,256]{2,1,0:T(2,128)}, f32[2,2,256]{2,1,0:T(2,128)S(1)}, f32[2,2,256,256]{3,2,0,1:T(8,128)S(1)}, bf16[256,1024]{0,1:T(8,128)...) while((s32[]{:T(128)}, f32[2,2,256]{2,1,0:T(2,128)}, ...), condition=%wide.region_19.20_spmd.clone.clone, body=%wide.region_12.19_spmd.clone.clone.sunk | while | flops 204019456 | bytes 10498871 | solution.py:119
  60.7 4.9 collective-permute-done
  73.3 4.9 collective-permute-done
  86.0 4.9 collective-permute-done
  98.7 4.9 collective-permute-done
  111.4 4.9 collective-permute-done
  118.1 4.4 collective-permute-start
  124.0 4.9 collective-permute-done
  136.7 4.9 collective-permute-done
  149.4 4.9 collective-permute-done
  162.1 4.9 collective-permute-done
  174.7 4.9 collective-permute-done
  187.4 4.9 collective-permute-done
  200.1 4.9 collective-permute-done
  212.8 4.9 collective-permute-done
  225.4 4.9 collective-permute-done
  238.1 4.9 collective-permute-done
  250.8 4.9 collective-permute-done
  263.5 4.9 collective-permute-done
  270.2 6.0 collective-permute-start
  277.8 4.9 collective-permute-done
  284.5 6.5 %collective-permute-start = (bf16[256,1024]{0,1:T(8,128)(2,1)}, bf16[256,1024]{0,1:T(8,128)(2,1)}, u32[]{:S(2)}, u32[]{:S(2)}) collective-permute-start(bf16[256,1024]{0,1:T(8,128)(2,1)} %copy.132), channel_id=1, source_target_pairs={{0,4},{4,8},{8,12},{12,16},{16,20},{20,24},{24,28},{28,32},{32,36}... | collective-permute-start | bytes 1572872 | tf_op jit(solution)/shard_map/while/body/eval_jaxpr/ppermute | solution.py:16
  292.5 4.9 collective-permute-done
  299.3 6.5 %collective-permute-start = (bf16[256,1024]{0,1:T(8,128)(2,1)}, bf16[256,1024]{0,1:T(8,128)(2,1)}, u32[]{:S(2)}, u32[]{:S(2)}) collective-permute-start(bf16[256,1024]{0,1:T(8,128)(2,1)} %copy.132), channel_id=1, source_target_pairs={{0,4},{4,8},{8,12},{12,16},{16,20},{20,24},{24,28},{28,32},{32,36}... | collective-permute-start | bytes 1572872 | tf_op jit(solution)/shard_map/while/body/eval_jaxpr/ppermute | solution.py:16
  307.3 4.9 collective-permute-done
  314.1 6.5 %collective-permute-start = (bf16[256,1024]{0,1:T(8,128)(2,1)}, bf16[256,1024]{0,1:T(8,128)(2,1)}, u32[]{:S(2)}, u32[]{:S(2)}) collective-permute-start(bf16[256,1024]{0,1:T(8,128)(2,1)} %copy.132), channel_id=1, source_target_pairs={{0,4},{4,8},{8,12},{12,16},{16,20},{20,24},{24,28},{28,32},{32,36}... | collective-permute-start | bytes 1572872 | tf_op jit(solution)/shard_map/while/body/eval_jaxpr/ppermute | solution.py:16
  322.1 4.9 collective-permute-done
  328.9 6.5 %collective-permute-start = (bf16[256,1024]{0,1:T(8,128)(2,1)}, bf16[256,1024]{0,1:T(8,128)(2,1)}, u32[]{:S(2)}, u32[]{:S(2)}) collective-permute-start(bf16[256,1024]{0,1:T(8,128)(2,1)} %copy.132), channel_id=1, source_target_pairs={{0,4},{4,8},{8,12},{12,16},{16,20},{20,24},{24,28},{28,32},{32,36}... | collective-permute-start | bytes 1572872 | tf_op jit(solution)/shard_map/while/body/eval_jaxpr/ppermute | solution.py:16
  336.9 4.9 collective-permute-done
  343.7 6.5 %collective-permute-start = (bf16[256,1024]{0,1:T(8,128)(2,1)}, bf16[256,1024]{0,1:T(8,128)(2,1)}, u32[]{:S(2)}, u32[]{:S(2)}) collective-permute-start(bf16[256,1024]{0,1:T(8,128)(2,1)} %copy.132), channel_id=1, source_target_pairs={{0,4},{4,8},{8,12},{12,16},{16,20},{20,24},{24,28},{28,32},{32,36}... | collective-permute-start | bytes 1572872 | tf_op jit(solution)/shard_map/while/body/eval_jaxpr/ppermute | solution.py:16
  351.7 4.9 collective-permute-done
  358.4 6.5 %collective-permute-start = (bf16[256,1024]{0,1:T(8,128)(2,1)}, bf16[256,1024]{0,1:T(8,128)(2,1)}, u32[]{:S(2)}, u32[]{:S(2)}) collective-permute-start(bf16[256,1024]{0,1:T(8,128)(2,1)} %copy.132), channel_id=1, source_target_pairs={{0,4},{4,8},{8,12},{12,16},{16,20},{20,24},{24,28},{28,32},{32,36}... | collective-permute-start | bytes 1572872 | tf_op jit(solution)/shard_map/while/body/eval_jaxpr/ppermute | solution.py:16
  366.5 4.9 collective-permute-done
  373.2 6.5 %collective-permute-start = (bf16[256,1024]{0,1:T(8,128)(2,1)}, bf16[256,1024]{0,1:T(8,128)(2,1)}, u32[]{:S(2)}, u32[]{:S(2)}) collective-permute-start(bf16[256,1024]{0,1:T(8,128)(2,1)} %copy.132), channel_id=1, source_target_pairs={{0,4},{4,8},{8,12},{12,16},{16,20},{20,24},{24,28},{28,32},{32,36}... | collective-permute-start | bytes 1572872 | tf_op jit(solution)/shard_map/while/body/eval_jaxpr/ppermute | solution.py:16
  381.2 4.9 collective-permute-done
  388.0 6.5 %collective-permute-start = (bf16[256,1024]{0,1:T(8,128)(2,1)}, bf16[256,1024]{0,1:T(8,128)(2,1)}, u32[]{:S(2)}, u32[]{:S(2)}) collective-permute-start(bf16[256,1024]{0,1:T(8,128)(2,1)} %copy.132), channel_id=1, source_target_pairs={{0,4},{4,8},{8,12},{12,16},{16,20},{20,24},{24,28},{28,32},{32,36}... | collective-permute-start | bytes 1572872 | tf_op jit(solution)/shard_map/while/body/eval_jaxpr/ppermute | solution.py:16
  396.0 4.9 collective-permute-done
  402.8 6.5 %collective-permute-start = (bf16[256,1024]{0,1:T(8,128)(2,1)}, bf16[256,1024]{0,1:T(8,128)(2,1)}, u32[]{:S(2)}, u32[]{:S(2)}) collective-permute-start(bf16[256,1024]{0,1:T(8,128)(2,1)} %copy.132), channel_id=1, source_target_pairs={{0,4},{4,8},{8,12},{12,16},{16,20},{20,24},{24,28},{28,32},{32,36}... | collective-permute-start | bytes 1572872 | tf_op jit(solution)/shard_map/while/body/eval_jaxpr/ppermute | solution.py:16
  410.8 4.9 collective-permute-done
  417.6 6.5 %collective-permute-start = (bf16[256,1024]{0,1:T(8,128)(2,1)}, bf16[256,1024]{0,1:T(8,128)(2,1)}, u32[]{:S(2)}, u32[]{:S(2)}) collective-permute-start(bf16[256,1024]{0,1:T(8,128)(2,1)} %copy.132), channel_id=1, source_target_pairs={{0,4},{4,8},{8,12},{12,16},{16,20},{20,24},{24,28},{28,32},{32,36}... | collective-permute-start | bytes 1572872 | tf_op jit(solution)/shard_map/while/body/eval_jaxpr/ppermute | solution.py:16
  425.6 4.9 collective-permute-done
  432.4 6.5 %collective-permute-start = (bf16[256,1024]{0,1:T(8,128)(2,1)}, bf16[256,1024]{0,1:T(8,128)(2,1)}, u32[]{:S(2)}, u32[]{:S(2)}) collective-permute-start(bf16[256,1024]{0,1:T(8,128)(2,1)} %copy.132), channel_id=1, source_target_pairs={{0,4},{4,8},{8,12},{12,16},{16,20},{20,24},{24,28},{28,32},{32,36}... | collective-permute-start | bytes 1572872 | tf_op jit(solution)/shard_map/while/body/eval_jaxpr/ppermute | solution.py:16
  440.4 4.9 collective-permute-done
  447.1 6.5 %collective-permute-start = (bf16[256,1024]{0,1:T(8,128)(2,1)}, bf16[256,1024]{0,1:T(8,128)(2,1)}, u32[]{:S(2)}, u32[]{:S(2)}) collective-permute-start(bf16[256,1024]{0,1:T(8,128)(2,1)} %copy.132), channel_id=1, source_target_pairs={{0,4},{4,8},{8,12},{12,16},{16,20},{20,24},{24,28},{28,32},{32,36}... | collective-permute-start | bytes 1572872 | tf_op jit(solution)/shard_map/while/body/eval_jaxpr/ppermute | solution.py:16
  455.2 4.9 collective-permute-done
  464.8 135.1 %all-reduce.2.cloned.1.call-done = bf16[256,2048]{1,0:T(8,128)(2,1)} async-done(((bf16[256,2048]{1,0:T(8,128)(2,1)}), bf16[256,2048]{1,0:T(8,128)(2,1)}) %all-reduce.2.cloned.1.call-update) | async-done | bytes 1048592 | tf_op jit(solution)/shard_map/psum | solution.py:131
  (321 shorter events, 205.4 us)
Async XLA Ops:
  7.2 455.9 %copy-start = (bf16[512,2048]{1,0:T(8,128)(2,1)S(1)}, bf16[512,2048]{1,0:T(8,128)(2,1)}, u32[]{:S(2)}) copy-start(bf16[512,2048]{1,0:T(8,128)(2,1)} %param.22) | copy-start | bytes 6291460
  7.2 592.7 %all-reduce.2.cloned.1.call-start = ((), (), s32[]{:S(2)}) async-start(), calls=%async_computation | async-start | bytes 2097152 | tf_op jit(solution)/shard_map/psum | solution.py:131
  10.6 2.7 copy-start.10
  14.4 4.1 copy-start.1
  14.9 0.6 copy-start.4
  15.7 5.3 copy-start.3
  18.4 2.6 copy-start.6
  18.4 8.0 %copy-start.11 = (f32[256]{0:T(256)S(1)}, f32[256]{0:T(256)}, u32[]{:S(2)}) copy-start(f32[256]{0:T(256)} %copy-done.10) | copy-start | bytes 3076
  18.4 8.0 %copy-start.12 = (bf16[2048,512]{1,0:T(8,128)(2,1)S(1)}, bf16[2048,512]{1,0:T(8,128)(2,1)}, u32[]{:S(2)}) copy-start(bf16[2048,512]{1,0:T(8,128)(2,1)} %param.19) | copy-start | bytes 6291460
  18.4 8.0 %copy-start.13 = (f32[2048]{0:T(1024)S(1)}, f32[2048]{0:T(1024)}, u32[]{:S(2)}) copy-start(f32[2048]{0:T(1024)} %param.18) | copy-start | bytes 24580
  21.0 5.4 copy-start.7
  21.9 18.7 %collective-permute-start.1 = (bf16[256,1024]{1,0:T(8,128)(2,1)}, bf16[256,1024]{1,0:T(8,128)(2,1)}, u32[]{:S(2)}, u32[]{:S(2)}) collective-permute-start(bf16[256,1024]{1,0:T(8,128)(2,1)} %pad_maximum_fusion), channel_id=1, source_target_pairs={{0,4},{4,8},{8,12},{12,16},{16,20},{20,24},{24,28},{28,32},{32,36}... | collective-permute-start | bytes 1572872 | tf_op jit(solution)/shard_map/ppermute | solution.py:16
  28.0 2.1 copy-start.5
  29.4 2.5 copy-start.14
  32.9 7.5 %copy-start.8 = (f32[4,2,128]{2,1,0:T(2,128)S(1)}, f32[4,2,128]{2,1,0:T(2,128)}, u32[]{:S(2)}) copy-start(f32[4,2,128]{2,1,0:T(2,128)} %param.23) | copy-start | bytes 12292
  44.5 8.4 %collective-permute-start = (bf16[256,1024]{0,1:T(8,128)(2,1)}, bf16[256,1024]{0,1:T(8,128)(2,1)}, u32[]{:S(2)}, u32[]{:S(2)}) collective-permute-start(bf16[256,1024]{0,1:T(8,128)(2,1)} %copy.132), channel_id=1, source_target_pairs={{0,4},{4,8},{8,12},{12,16},{16,20},{20,24},{24,28},{28,32},{32,36}... | collective-permute-start | bytes 1572872 | tf_op jit(solution)/shard_map/while/body/eval_jaxpr/ppermute | solution.py:16
  54.8 10.8 %collective-permute-start = (bf16[256,1024]{0,1:T(8,128)(2,1)}, bf16[256,1024]{0,1:T(8,128)(2,1)}, u32[]{:S(2)}, u32[]{:S(2)}) collective-permute-start(bf16[256,1024]{0,1:T(8,128)(2,1)} %copy.132), channel_id=1, source_target_pairs={{0,4},{4,8},{8,12},{12,16},{16,20},{20,24},{24,28},{28,32},{32,36}... | collective-permute-start | bytes 1572872 | tf_op jit(solution)/shard_map/while/body/eval_jaxpr/ppermute | solution.py:16
  67.4 10.8 %collective-permute-start = (bf16[256,1024]{0,1:T(8,128)(2,1)}, bf16[256,1024]{0,1:T(8,128)(2,1)}, u32[]{:S(2)}, u32[]{:S(2)}) collective-permute-start(bf16[256,1024]{0,1:T(8,128)(2,1)} %copy.132), channel_id=1, source_target_pairs={{0,4},{4,8},{8,12},{12,16},{16,20},{20,24},{24,28},{28,32},{32,36}... | collective-permute-start | bytes 1572872 | tf_op jit(solution)/shard_map/while/body/eval_jaxpr/ppermute | solution.py:16
  80.1 10.8 %collective-permute-start = (bf16[256,1024]{0,1:T(8,128)(2,1)}, bf16[256,1024]{0,1:T(8,128)(2,1)}, u32[]{:S(2)}, u32[]{:S(2)}) collective-permute-start(bf16[256,1024]{0,1:T(8,128)(2,1)} %copy.132), channel_id=1, source_target_pairs={{0,4},{4,8},{8,12},{12,16},{16,20},{20,24},{24,28},{28,32},{32,36}... | collective-permute-start | bytes 1572872 | tf_op jit(solution)/shard_map/while/body/eval_jaxpr/ppermute | solution.py:16
  92.8 10.8 %collective-permute-start = (bf16[256,1024]{0,1:T(8,128)(2,1)}, bf16[256,1024]{0,1:T(8,128)(2,1)}, u32[]{:S(2)}, u32[]{:S(2)}) collective-permute-start(bf16[256,1024]{0,1:T(8,128)(2,1)} %copy.132), channel_id=1, source_target_pairs={{0,4},{4,8},{8,12},{12,16},{16,20},{20,24},{24,28},{28,32},{32,36}... | collective-permute-start | bytes 1572872 | tf_op jit(solution)/shard_map/while/body/eval_jaxpr/ppermute | solution.py:16
  105.5 10.8 %collective-permute-start = (bf16[256,1024]{0,1:T(8,128)(2,1)}, bf16[256,1024]{0,1:T(8,128)(2,1)}, u32[]{:S(2)}, u32[]{:S(2)}) collective-permute-start(bf16[256,1024]{0,1:T(8,128)(2,1)} %copy.132), channel_id=1, source_target_pairs={{0,4},{4,8},{8,12},{12,16},{16,20},{20,24},{24,28},{28,32},{32,36}... | collective-permute-start | bytes 1572872 | tf_op jit(solution)/shard_map/while/body/eval_jaxpr/ppermute | solution.py:16
  118.1 10.8 %collective-permute-start = (bf16[256,1024]{0,1:T(8,128)(2,1)}, bf16[256,1024]{0,1:T(8,128)(2,1)}, u32[]{:S(2)}, u32[]{:S(2)}) collective-permute-start(bf16[256,1024]{0,1:T(8,128)(2,1)} %copy.132), channel_id=1, source_target_pairs={{0,4},{4,8},{8,12},{12,16},{16,20},{20,24},{24,28},{28,32},{32,36}... | collective-permute-start | bytes 1572872 | tf_op jit(solution)/shard_map/while/body/eval_jaxpr/ppermute | solution.py:16
  130.8 10.8 %collective-permute-start = (bf16[256,1024]{0,1:T(8,128)(2,1)}, bf16[256,1024]{0,1:T(8,128)(2,1)}, u32[]{:S(2)}, u32[]{:S(2)}) collective-permute-start(bf16[256,1024]{0,1:T(8,128)(2,1)} %copy.132), channel_id=1, source_target_pairs={{0,4},{4,8},{8,12},{12,16},{16,20},{20,24},{24,28},{28,32},{32,36}... | collective-permute-start | bytes 1572872 | tf_op jit(solution)/shard_map/while/body/eval_jaxpr/ppermute | solution.py:16
  143.5 10.8 %collective-permute-start = (bf16[256,1024]{0,1:T(8,128)(2,1)}, bf16[256,1024]{0,1:T(8,128)(2,1)}, u32[]{:S(2)}, u32[]{:S(2)}) collective-permute-start(bf16[256,1024]{0,1:T(8,128)(2,1)} %copy.132), channel_id=1, source_target_pairs={{0,4},{4,8},{8,12},{12,16},{16,20},{20,24},{24,28},{28,32},{32,36}... | collective-permute-start | bytes 1572872 | tf_op jit(solution)/shard_map/while/body/eval_jaxpr/ppermute | solution.py:16
  156.2 10.8 %collective-permute-start = (bf16[256,1024]{0,1:T(8,128)(2,1)}, bf16[256,1024]{0,1:T(8,128)(2,1)}, u32[]{:S(2)}, u32[]{:S(2)}) collective-permute-start(bf16[256,1024]{0,1:T(8,128)(2,1)} %copy.132), channel_id=1, source_target_pairs={{0,4},{4,8},{8,12},{12,16},{16,20},{20,24},{24,28},{28,32},{32,36}... | collective-permute-start | bytes 1572872 | tf_op jit(solution)/shard_map/while/body/eval_jaxpr/ppermute | solution.py:16
  168.8 10.8 %collective-permute-start = (bf16[256,1024]{0,1:T(8,128)(2,1)}, bf16[256,1024]{0,1:T(8,128)(2,1)}, u32[]{:S(2)}, u32[]{:S(2)}) collective-permute-start(bf16[256,1024]{0,1:T(8,128)(2,1)} %copy.132), channel_id=1, source_target_pairs={{0,4},{4,8},{8,12},{12,16},{16,20},{20,24},{24,28},{28,32},{32,36}... | collective-permute-start | bytes 1572872 | tf_op jit(solution)/shard_map/while/body/eval_jaxpr/ppermute | solution.py:16
  181.5 10.8 %collective-permute-start = (bf16[256,1024]{0,1:T(8,128)(2,1)}, bf16[256,1024]{0,1:T(8,128)(2,1)}, u32[]{:S(2)}, u32[]{:S(2)}) collective-permute-start(bf16[256,1024]{0,1:T(8,128)(2,1)} %copy.132), channel_id=1, source_target_pairs={{0,4},{4,8},{8,12},{12,16},{16,20},{20,24},{24,28},{28,32},{32,36}... | collective-permute-start | bytes 1572872 | tf_op jit(solution)/shard_map/while/body/eval_jaxpr/ppermute | solution.py:16
  194.2 10.8 %collective-permute-start = (bf16[256,1024]{0,1:T(8,128)(2,1)}, bf16[256,1024]{0,1:T(8,128)(2,1)}, u32[]{:S(2)}, u32[]{:S(2)}) collective-permute-start(bf16[256,1024]{0,1:T(8,128)(2,1)} %copy.132), channel_id=1, source_target_pairs={{0,4},{4,8},{8,12},{12,16},{16,20},{20,24},{24,28},{28,32},{32,36}... | collective-permute-start | bytes 1572872 | tf_op jit(solution)/shard_map/while/body/eval_jaxpr/ppermute | solution.py:16
  206.9 10.8 %collective-permute-start = (bf16[256,1024]{0,1:T(8,128)(2,1)}, bf16[256,1024]{0,1:T(8,128)(2,1)}, u32[]{:S(2)}, u32[]{:S(2)}) collective-permute-start(bf16[256,1024]{0,1:T(8,128)(2,1)} %copy.132), channel_id=1, source_target_pairs={{0,4},{4,8},{8,12},{12,16},{16,20},{20,24},{24,28},{28,32},{32,36}... | collective-permute-start | bytes 1572872 | tf_op jit(solution)/shard_map/while/body/eval_jaxpr/ppermute | solution.py:16
  219.5 10.8 %collective-permute-start = (bf16[256,1024]{0,1:T(8,128)(2,1)}, bf16[256,1024]{0,1:T(8,128)(2,1)}, u32[]{:S(2)}, u32[]{:S(2)}) collective-permute-start(bf16[256,1024]{0,1:T(8,128)(2,1)} %copy.132), channel_id=1, source_target_pairs={{0,4},{4,8},{8,12},{12,16},{16,20},{20,24},{24,28},{28,32},{32,36}... | collective-permute-start | bytes 1572872 | tf_op jit(solution)/shard_map/while/body/eval_jaxpr/ppermute | solution.py:16
  232.2 10.8 %collective-permute-start = (bf16[256,1024]{0,1:T(8,128)(2,1)}, bf16[256,1024]{0,1:T(8,128)(2,1)}, u32[]{:S(2)}, u32[]{:S(2)}) collective-permute-start(bf16[256,1024]{0,1:T(8,128)(2,1)} %copy.132), channel_id=1, source_target_pairs={{0,4},{4,8},{8,12},{12,16},{16,20},{20,24},{24,28},{28,32},{32,36}... | collective-permute-start | bytes 1572872 | tf_op jit(solution)/shard_map/while/body/eval_jaxpr/ppermute | solution.py:16
  244.9 10.8 %collective-permute-start = (bf16[256,1024]{0,1:T(8,128)(2,1)}, bf16[256,1024]{0,1:T(8,128)(2,1)}, u32[]{:S(2)}, u32[]{:S(2)}) collective-permute-start(bf16[256,1024]{0,1:T(8,128)(2,1)} %copy.132), channel_id=1, source_target_pairs={{0,4},{4,8},{8,12},{12,16},{16,20},{20,24},{24,28},{28,32},{32,36}... | collective-permute-start | bytes 1572872 | tf_op jit(solution)/shard_map/while/body/eval_jaxpr/ppermute | solution.py:16
  257.6 10.8 %collective-permute-start = (bf16[256,1024]{0,1:T(8,128)(2,1)}, bf16[256,1024]{0,1:T(8,128)(2,1)}, u32[]{:S(2)}, u32[]{:S(2)}) collective-permute-start(bf16[256,1024]{0,1:T(8,128)(2,1)} %copy.132), channel_id=1, source_target_pairs={{0,4},{4,8},{8,12},{12,16},{16,20},{20,24},{24,28},{28,32},{32,36}... | collective-permute-start | bytes 1572872 | tf_op jit(solution)/shard_map/while/body/eval_jaxpr/ppermute | solution.py:16
  270.2 12.4 %collective-permute-start = (bf16[256,1024]{0,1:T(8,128)(2,1)}, bf16[256,1024]{0,1:T(8,128)(2,1)}, u32[]{:S(2)}, u32[]{:S(2)}) collective-permute-start(bf16[256,1024]{0,1:T(8,128)(2,1)} %copy.132), channel_id=1, source_target_pairs={{0,4},{4,8},{8,12},{12,16},{16,20},{20,24},{24,28},{28,32},{32,36}... | collective-permute-start | bytes 1572872 | tf_op jit(solution)/shard_map/while/body/eval_jaxpr/ppermute | solution.py:16
  284.5 12.9 %collective-permute-start = (bf16[256,1024]{0,1:T(8,128)(2,1)}, bf16[256,1024]{0,1:T(8,128)(2,1)}, u32[]{:S(2)}, u32[]{:S(2)}) collective-permute-start(bf16[256,1024]{0,1:T(8,128)(2,1)} %copy.132), channel_id=1, source_target_pairs={{0,4},{4,8},{8,12},{12,16},{16,20},{20,24},{24,28},{28,32},{32,36}... | collective-permute-start | bytes 1572872 | tf_op jit(solution)/shard_map/while/body/eval_jaxpr/ppermute | solution.py:16
  299.3 12.9 %collective-permute-start = (bf16[256,1024]{0,1:T(8,128)(2,1)}, bf16[256,1024]{0,1:T(8,128)(2,1)}, u32[]{:S(2)}, u32[]{:S(2)}) collective-permute-start(bf16[256,1024]{0,1:T(8,128)(2,1)} %copy.132), channel_id=1, source_target_pairs={{0,4},{4,8},{8,12},{12,16},{16,20},{20,24},{24,28},{28,32},{32,36}... | collective-permute-start | bytes 1572872 | tf_op jit(solution)/shard_map/while/body/eval_jaxpr/ppermute | solution.py:16
  314.1 12.9 %collective-permute-start = (bf16[256,1024]{0,1:T(8,128)(2,1)}, bf16[256,1024]{0,1:T(8,128)(2,1)}, u32[]{:S(2)}, u32[]{:S(2)}) collective-permute-start(bf16[256,1024]{0,1:T(8,128)(2,1)} %copy.132), channel_id=1, source_target_pairs={{0,4},{4,8},{8,12},{12,16},{16,20},{20,24},{24,28},{28,32},{32,36}... | collective-permute-start | bytes 1572872 | tf_op jit(solution)/shard_map/while/body/eval_jaxpr/ppermute | solution.py:16
  328.9 12.9 %collective-permute-start = (bf16[256,1024]{0,1:T(8,128)(2,1)}, bf16[256,1024]{0,1:T(8,128)(2,1)}, u32[]{:S(2)}, u32[]{:S(2)}) collective-permute-start(bf16[256,1024]{0,1:T(8,128)(2,1)} %copy.132), channel_id=1, source_target_pairs={{0,4},{4,8},{8,12},{12,16},{16,20},{20,24},{24,28},{28,32},{32,36}... | collective-permute-start | bytes 1572872 | tf_op jit(solution)/shard_map/while/body/eval_jaxpr/ppermute | solution.py:16
  343.7 12.9 %collective-permute-start = (bf16[256,1024]{0,1:T(8,128)(2,1)}, bf16[256,1024]{0,1:T(8,128)(2,1)}, u32[]{:S(2)}, u32[]{:S(2)}) collective-permute-start(bf16[256,1024]{0,1:T(8,128)(2,1)} %copy.132), channel_id=1, source_target_pairs={{0,4},{4,8},{8,12},{12,16},{16,20},{20,24},{24,28},{28,32},{32,36}... | collective-permute-start | bytes 1572872 | tf_op jit(solution)/shard_map/while/body/eval_jaxpr/ppermute | solution.py:16
  358.4 12.9 %collective-permute-start = (bf16[256,1024]{0,1:T(8,128)(2,1)}, bf16[256,1024]{0,1:T(8,128)(2,1)}, u32[]{:S(2)}, u32[]{:S(2)}) collective-permute-start(bf16[256,1024]{0,1:T(8,128)(2,1)} %copy.132), channel_id=1, source_target_pairs={{0,4},{4,8},{8,12},{12,16},{16,20},{20,24},{24,28},{28,32},{32,36}... | collective-permute-start | bytes 1572872 | tf_op jit(solution)/shard_map/while/body/eval_jaxpr/ppermute | solution.py:16
  373.2 12.9 %collective-permute-start = (bf16[256,1024]{0,1:T(8,128)(2,1)}, bf16[256,1024]{0,1:T(8,128)(2,1)}, u32[]{:S(2)}, u32[]{:S(2)}) collective-permute-start(bf16[256,1024]{0,1:T(8,128)(2,1)} %copy.132), channel_id=1, source_target_pairs={{0,4},{4,8},{8,12},{12,16},{16,20},{20,24},{24,28},{28,32},{32,36}... | collective-permute-start | bytes 1572872 | tf_op jit(solution)/shard_map/while/body/eval_jaxpr/ppermute | solution.py:16
  388.0 12.9 %collective-permute-start = (bf16[256,1024]{0,1:T(8,128)(2,1)}, bf16[256,1024]{0,1:T(8,128)(2,1)}, u32[]{:S(2)}, u32[]{:S(2)}) collective-permute-start(bf16[256,1024]{0,1:T(8,128)(2,1)} %copy.132), channel_id=1, source_target_pairs={{0,4},{4,8},{8,12},{12,16},{16,20},{20,24},{24,28},{28,32},{32,36}... | collective-permute-start | bytes 1572872 | tf_op jit(solution)/shard_map/while/body/eval_jaxpr/ppermute | solution.py:16
  402.8 12.9 %collective-permute-start = (bf16[256,1024]{0,1:T(8,128)(2,1)}, bf16[256,1024]{0,1:T(8,128)(2,1)}, u32[]{:S(2)}, u32[]{:S(2)}) collective-permute-start(bf16[256,1024]{0,1:T(8,128)(2,1)} %copy.132), channel_id=1, source_target_pairs={{0,4},{4,8},{8,12},{12,16},{16,20},{20,24},{24,28},{28,32},{32,36}... | collective-permute-start | bytes 1572872 | tf_op jit(solution)/shard_map/while/body/eval_jaxpr/ppermute | solution.py:16
  417.6 12.9 %collective-permute-start = (bf16[256,1024]{0,1:T(8,128)(2,1)}, bf16[256,1024]{0,1:T(8,128)(2,1)}, u32[]{:S(2)}, u32[]{:S(2)}) collective-permute-start(bf16[256,1024]{0,1:T(8,128)(2,1)} %copy.132), channel_id=1, source_target_pairs={{0,4},{4,8},{8,12},{12,16},{16,20},{20,24},{24,28},{28,32},{32,36}... | collective-permute-start | bytes 1572872 | tf_op jit(solution)/shard_map/while/body/eval_jaxpr/ppermute | solution.py:16
  432.4 12.9 %collective-permute-start = (bf16[256,1024]{0,1:T(8,128)(2,1)}, bf16[256,1024]{0,1:T(8,128)(2,1)}, u32[]{:S(2)}, u32[]{:S(2)}) collective-permute-start(bf16[256,1024]{0,1:T(8,128)(2,1)} %copy.132), channel_id=1, source_target_pairs={{0,4},{4,8},{8,12},{12,16},{16,20},{20,24},{24,28},{28,32},{32,36}... | collective-permute-start | bytes 1572872 | tf_op jit(solution)/shard_map/while/body/eval_jaxpr/ppermute | solution.py:16
  447.1 12.9 %collective-permute-start = (bf16[256,1024]{0,1:T(8,128)(2,1)}, bf16[256,1024]{0,1:T(8,128)(2,1)}, u32[]{:S(2)}, u32[]{:S(2)}) collective-permute-start(bf16[256,1024]{0,1:T(8,128)(2,1)} %copy.132), channel_id=1, source_target_pairs={{0,4},{4,8},{8,12},{12,16},{16,20},{20,24},{24,28},{28,32},{32,36}... | collective-permute-start | bytes 1572872 | tf_op jit(solution)/shard_map/while/body/eval_jaxpr/ppermute | solution.py:16
  461.4 1.5 copy-start.9
  463.1 136.9 %copy-start.2 = (bf16[256,2048]{1,0:T(8,128)(2,1)S(1)}, bf16[256,2048]{1,0:T(8,128)(2,1)}, u32[]{:S(2)}) copy-start(bf16[256,2048]{1,0:T(8,128)(2,1)} %param.17) | copy-start | bytes 3145732
Sparse Core Ops, SparseCore 0:
  464.9 134.9 all-reduce.1
where the time goes:
time: 615 us; the launch traced here: 609 us
  waiting for transfers between devices  283 us (46%)
  starting transfers between devices  165 us (27%)
  local copies, waits for them, and re-layouts  71.1 us (12%)
  other arithmetic  43.3 us (7%)
  loops' own time  19.5 us (3%)
  between operations  15.7 us (3%)
  matrix products  12.3 us (2%)
    ppermute x32, starting transfers between devices, shifted(): lax.ppermute(value, axis, [(source, source + steps) for source in range(f...  165 us
    ppermute x32, waiting for transfers between devices, shifted(): lax.ppermute(value, axis, [(source, source + steps) for source in range(f...  148 us
    psum x1, waiting for transfers between devices, on_device(): lax.psum(jnp.dot(merged, w_out, preferred_element_type=jnp.float32).astyp...  135 us
    while x31, local copies, waits for them, and re-layouts  57.9 us
    reduce_or x31, other arithmetic, absorb(): return lax.cond(jnp.any(allowed), compute, keep, state)  24.8 us
    another operation x1, loops' own time, on_device(): state, moving = lax.fori_loop(0, reach - 1, turn, (state, arriving))  19 us
  transfers between devices with their start and end apart: 33, of which 32 were waited for; matrix products, arithmetic and copies ran while one was open for 7% of the time, Pallas kernels for 0%

commit v1 on v0

--- a/solution.py
+++ b/solution.py
@@ -128,8 +128,13 @@
         * (1.0 - lambda_start)
     )
     merged = jnp.transpose(normed_heads, (1, 0, 2)).reshape(rows, heads * VD).astype(jnp.bfloat16)
-    summed = lax.psum(
-        jnp.dot(merged, w_out, preferred_element_type=jnp.float32).astype(jnp.bfloat16), "tp"
+
+    def _follow_cards(page):
+        main = lax.all_gather(page, "tp").sum(axis=0)
+        return main
+
+    summed = _follow_cards(
+        jnp.dot(merged, w_out, preferred_element_type=jnp.float32).astype(jnp.bfloat16)
     ).astype(jnp.float32)
     hidden = (xf + summed).astype(jnp.bfloat16)
     return (hidden, key_flat, values)

time: 615 us -> 640 us (1.041)
  the two profiles are of different devices: /device:TPU:1 before, /device:TPU:37 now
where the time goes in v1:
time: 640 us; the launch traced here: 634 us
  starting transfers between devices  213 us (33%)
  waiting for transfers between devices  201 us (31%)
  local copies, waits for them, and re-layouts  92.2 us (14%)
  other arithmetic  67.6 us (11%)
  matrix products  25.3 us (4%)
  loops' own time  19.7 us (3%)
  between operations  15.6 us (2%)
    ppermute x32, starting transfers between devices, shifted(): lax.ppermute(value, axis, [(source, source + steps) for source in range(f...  213 us
    all_gather x1, waiting for transfers between devices, _follow_cards(): main = lax.all_gather(page, 'tp').sum(axis=0)  106 us
    ppermute x32, waiting for transfers between devices, shifted(): lax.ppermute(value, axis, [(source, source + steps) for source in range(f...  95.7 us
    while x31, local copies, waits for them, and re-layouts  57.9 us
    reduce_or x31, other arithmetic, absorb(): return lax.cond(jnp.any(allowed), compute, keep, state)  24.8 us
    another operation x1, loops' own time, on_device(): state, moving = lax.fori_loop(0, reach - 1, turn, (state, arriving))  19 us
    slice x13, local copies, waits for them, and re-layouts, compute(): shard_values = shard[:, key_cols:].reshape(rows, heads, VD)  13.9 us
  transfers between devices with their start and end apart: 33, of which 32 were waited for; matrix products, arithmetic and copies ran while one was open for 15% of the time, Pallas kernels for 0%

profile of v1, /device:TPU:37, one launch (start us, length us, event | category | flops | bytes accessed | tf_op | source)
XLA Modules:
  0.0 634.2 jit_solution(6324126706851802144)
XLA Ops:
  35.9 5.7 conditional.3
  43.8 466.3 %while.23 = (s32[]{:T(128)}, f32[2,2,256]{2,1,0:T(2,128)}, f32[2,2,256]{2,1,0:T(2,128)S(1)}, f32[2,2,256,256]{3,2,0,1:T(8,128)S(1)}, bf16[256,1024]{0,1:T(8,128)...) while((s32[]{:T(128)}, f32[2,2,256]{2,1,0:T(2,128)}, ...), condition=%wide.region_19.20_spmd.clone.clone, body=%wide.region_12.19_spmd.clone.clone.sunk | while | flops 204019456 | bytes 10498871 | solution.py:119
  93.9 6.0 collective-permute-start
  108.3 7.4 %collective-permute-start = (bf16[256,1024]{0,1:T(8,128)(2,1)}, bf16[256,1024]{0,1:T(8,128)(2,1)}, u32[]{:S(2)}, u32[]{:S(2)}) collective-permute-start(bf16[256,1024]{0,1:T(8,128)(2,1)} %copy.132), channel_id=1, source_target_pairs={{0,4},{4,8},{8,12},{12,16},{16,20},{20,24},{24,28},{28,32},{32,36}... | collective-permute-start | bytes 1572872 | tf_op jit(solution)/shard_map/while/body/eval_jaxpr/ppermute | solution.py:16
  124.0 7.4 %collective-permute-start = (bf16[256,1024]{0,1:T(8,128)(2,1)}, bf16[256,1024]{0,1:T(8,128)(2,1)}, u32[]{:S(2)}, u32[]{:S(2)}) collective-permute-start(bf16[256,1024]{0,1:T(8,128)(2,1)} %copy.132), channel_id=1, source_target_pairs={{0,4},{4,8},{8,12},{12,16},{16,20},{20,24},{24,28},{28,32},{32,36}... | collective-permute-start | bytes 1572872 | tf_op jit(solution)/shard_map/while/body/eval_jaxpr/ppermute | solution.py:16
  139.6 7.4 %collective-permute-start = (bf16[256,1024]{0,1:T(8,128)(2,1)}, bf16[256,1024]{0,1:T(8,128)(2,1)}, u32[]{:S(2)}, u32[]{:S(2)}) collective-permute-start(bf16[256,1024]{0,1:T(8,128)(2,1)} %copy.132), channel_id=1, source_target_pairs={{0,4},{4,8},{8,12},{12,16},{16,20},{20,24},{24,28},{28,32},{32,36}... | collective-permute-start | bytes 1572872 | tf_op jit(solution)/shard_map/while/body/eval_jaxpr/ppermute | solution.py:16
  155.3 7.4 %collective-permute-start = (bf16[256,1024]{0,1:T(8,128)(2,1)}, bf16[256,1024]{0,1:T(8,128)(2,1)}, u32[]{:S(2)}, u32[]{:S(2)}) collective-permute-start(bf16[256,1024]{0,1:T(8,128)(2,1)} %copy.132), channel_id=1, source_target_pairs={{0,4},{4,8},{8,12},{12,16},{16,20},{20,24},{24,28},{28,32},{32,36}... | collective-permute-start | bytes 1572872 | tf_op jit(solution)/shard_map/while/body/eval_jaxpr/ppermute | solution.py:16
  171.0 7.4 %collective-permute-start = (bf16[256,1024]{0,1:T(8,128)(2,1)}, bf16[256,1024]{0,1:T(8,128)(2,1)}, u32[]{:S(2)}, u32[]{:S(2)}) collective-permute-start(bf16[256,1024]{0,1:T(8,128)(2,1)} %copy.132), channel_id=1, source_target_pairs={{0,4},{4,8},{8,12},{12,16},{16,20},{20,24},{24,28},{28,32},{32,36}... | collective-permute-start | bytes 1572872 | tf_op jit(solution)/shard_map/while/body/eval_jaxpr/ppermute | solution.py:16
  186.7 7.4 %collective-permute-start = (bf16[256,1024]{0,1:T(8,128)(2,1)}, bf16[256,1024]{0,1:T(8,128)(2,1)}, u32[]{:S(2)}, u32[]{:S(2)}) collective-permute-start(bf16[256,1024]{0,1:T(8,128)(2,1)} %copy.132), channel_id=1, source_target_pairs={{0,4},{4,8},{8,12},{12,16},{16,20},{20,24},{24,28},{28,32},{32,36}... | collective-permute-start | bytes 1572872 | tf_op jit(solution)/shard_map/while/body/eval_jaxpr/ppermute | solution.py:16
  202.4 7.4 %collective-permute-start = (bf16[256,1024]{0,1:T(8,128)(2,1)}, bf16[256,1024]{0,1:T(8,128)(2,1)}, u32[]{:S(2)}, u32[]{:S(2)}) collective-permute-start(bf16[256,1024]{0,1:T(8,128)(2,1)} %copy.132), channel_id=1, source_target_pairs={{0,4},{4,8},{8,12},{12,16},{16,20},{20,24},{24,28},{28,32},{32,36}... | collective-permute-start | bytes 1572872 | tf_op jit(solution)/shard_map/while/body/eval_jaxpr/ppermute | solution.py:16
  218.0 7.4 %collective-permute-start = (bf16[256,1024]{0,1:T(8,128)(2,1)}, bf16[256,1024]{0,1:T(8,128)(2,1)}, u32[]{:S(2)}, u32[]{:S(2)}) collective-permute-start(bf16[256,1024]{0,1:T(8,128)(2,1)} %copy.132), channel_id=1, source_target_pairs={{0,4},{4,8},{8,12},{12,16},{16,20},{20,24},{24,28},{28,32},{32,36}... | collective-permute-start | bytes 1572872 | tf_op jit(solution)/shard_map/while/body/eval_jaxpr/ppermute | solution.py:16
  233.7 7.4 %collective-permute-start = (bf16[256,1024]{0,1:T(8,128)(2,1)}, bf16[256,1024]{0,1:T(8,128)(2,1)}, u32[]{:S(2)}, u32[]{:S(2)}) collective-permute-start(bf16[256,1024]{0,1:T(8,128)(2,1)} %copy.132), channel_id=1, source_target_pairs={{0,4},{4,8},{8,12},{12,16},{16,20},{20,24},{24,28},{28,32},{32,36}... | collective-permute-start | bytes 1572872 | tf_op jit(solution)/shard_map/while/body/eval_jaxpr/ppermute | solution.py:16
  242.6 4.9 collective-permute-done
  249.4 7.4 %collective-permute-start = (bf16[256,1024]{0,1:T(8,128)(2,1)}, bf16[256,1024]{0,1:T(8,128)(2,1)}, u32[]{:S(2)}, u32[]{:S(2)}) collective-permute-start(bf16[256,1024]{0,1:T(8,128)(2,1)} %copy.132), channel_id=1, source_target_pairs={{0,4},{4,8},{8,12},{12,16},{16,20},{20,24},{24,28},{28,32},{32,36}... | collective-permute-start | bytes 1572872 | tf_op jit(solution)/shard_map/while/body/eval_jaxpr/ppermute | solution.py:16
  258.3 4.9 collective-permute-done
  265.1 4.4 collective-permute-start
  271.0 4.9 collective-permute-done
  277.8 6.4 %collective-permute-start = (bf16[256,1024]{0,1:T(8,128)(2,1)}, bf16[256,1024]{0,1:T(8,128)(2,1)}, u32[]{:S(2)}, u32[]{:S(2)}) collective-permute-start(bf16[256,1024]{0,1:T(8,128)(2,1)} %copy.132), channel_id=1, source_target_pairs={{0,4},{4,8},{8,12},{12,16},{16,20},{20,24},{24,28},{28,32},{32,36}... | collective-permute-start | bytes 1572872 | tf_op jit(solution)/shard_map/while/body/eval_jaxpr/ppermute | solution.py:16
  285.7 4.9 collective-permute-done
  292.4 7.4 %collective-permute-start = (bf16[256,1024]{0,1:T(8,128)(2,1)}, bf16[256,1024]{0,1:T(8,128)(2,1)}, u32[]{:S(2)}, u32[]{:S(2)}) collective-permute-start(bf16[256,1024]{0,1:T(8,128)(2,1)} %copy.132), channel_id=1, source_target_pairs={{0,4},{4,8},{8,12},{12,16},{16,20},{20,24},{24,28},{28,32},{32,36}... | collective-permute-start | bytes 1572872 | tf_op jit(solution)/shard_map/while/body/eval_jaxpr/ppermute | solution.py:16
  301.4 4.9 collective-permute-done
  308.1 7.4 %collective-permute-start = (bf16[256,1024]{0,1:T(8,128)(2,1)}, bf16[256,1024]{0,1:T(8,128)(2,1)}, u32[]{:S(2)}, u32[]{:S(2)}) collective-permute-start(bf16[256,1024]{0,1:T(8,128)(2,1)} %copy.132), channel_id=1, source_target_pairs={{0,4},{4,8},{8,12},{12,16},{16,20},{20,24},{24,28},{28,32},{32,36}... | collective-permute-start | bytes 1572872 | tf_op jit(solution)/shard_map/while/body/eval_jaxpr/ppermute | solution.py:16
  317.0 4.9 collective-permute-done
  323.8 7.4 %collective-permute-start = (bf16[256,1024]{0,1:T(8,128)(2,1)}, bf16[256,1024]{0,1:T(8,128)(2,1)}, u32[]{:S(2)}, u32[]{:S(2)}) collective-permute-start(bf16[256,1024]{0,1:T(8,128)(2,1)} %copy.132), channel_id=1, source_target_pairs={{0,4},{4,8},{8,12},{12,16},{16,20},{20,24},{24,28},{28,32},{32,36}... | collective-permute-start | bytes 1572872 | tf_op jit(solution)/shard_map/while/body/eval_jaxpr/ppermute | solution.py:16
  332.7 4.9 collective-permute-done
  339.5 7.4 %collective-permute-start = (bf16[256,1024]{0,1:T(8,128)(2,1)}, bf16[256,1024]{0,1:T(8,128)(2,1)}, u32[]{:S(2)}, u32[]{:S(2)}) collective-permute-start(bf16[256,1024]{0,1:T(8,128)(2,1)} %copy.132), channel_id=1, source_target_pairs={{0,4},{4,8},{8,12},{12,16},{16,20},{20,24},{24,28},{28,32},{32,36}... | collective-permute-start | bytes 1572872 | tf_op jit(solution)/shard_map/while/body/eval_jaxpr/ppermute | solution.py:16
  348.4 4.9 collective-permute-done
  355.2 7.4 %collective-permute-start = (bf16[256,1024]{0,1:T(8,128)(2,1)}, bf16[256,1024]{0,1:T(8,128)(2,1)}, u32[]{:S(2)}, u32[]{:S(2)}) collective-permute-start(bf16[256,1024]{0,1:T(8,128)(2,1)} %copy.132), channel_id=1, source_target_pairs={{0,4},{4,8},{8,12},{12,16},{16,20},{20,24},{24,28},{28,32},{32,36}... | collective-permute-start | bytes 1572872 | tf_op jit(solution)/shard_map/while/body/eval_jaxpr/ppermute | solution.py:16
  364.1 4.9 collective-permute-done
  370.9 7.4 %collective-permute-start = (bf16[256,1024]{0,1:T(8,128)(2,1)}, bf16[256,1024]{0,1:T(8,128)(2,1)}, u32[]{:S(2)}, u32[]{:S(2)}) collective-permute-start(bf16[256,1024]{0,1:T(8,128)(2,1)} %copy.132), channel_id=1, source_target_pairs={{0,4},{4,8},{8,12},{12,16},{16,20},{20,24},{24,28},{28,32},{32,36}... | collective-permute-start | bytes 1572872 | tf_op jit(solution)/shard_map/while/body/eval_jaxpr/ppermute | solution.py:16
  379.8 4.9 collective-permute-done
  386.5 7.4 %collective-permute-start = (bf16[256,1024]{0,1:T(8,128)(2,1)}, bf16[256,1024]{0,1:T(8,128)(2,1)}, u32[]{:S(2)}, u32[]{:S(2)}) collective-permute-start(bf16[256,1024]{0,1:T(8,128)(2,1)} %copy.132), channel_id=1, source_target_pairs={{0,4},{4,8},{8,12},{12,16},{16,20},{20,24},{24,28},{28,32},{32,36}... | collective-permute-start | bytes 1572872 | tf_op jit(solution)/shard_map/while/body/eval_jaxpr/ppermute | solution.py:16
  395.5 4.9 collective-permute-done
  402.2 7.4 %collective-permute-start = (bf16[256,1024]{0,1:T(8,128)(2,1)}, bf16[256,1024]{0,1:T(8,128)(2,1)}, u32[]{:S(2)}, u32[]{:S(2)}) collective-permute-start(bf16[256,1024]{0,1:T(8,128)(2,1)} %copy.132), channel_id=1, source_target_pairs={{0,4},{4,8},{8,12},{12,16},{16,20},{20,24},{24,28},{28,32},{32,36}... | collective-permute-start | bytes 1572872 | tf_op jit(solution)/shard_map/while/body/eval_jaxpr/ppermute | solution.py:16
  411.1 4.9 collective-permute-done
  417.9 7.4 %collective-permute-start = (bf16[256,1024]{0,1:T(8,128)(2,1)}, bf16[256,1024]{0,1:T(8,128)(2,1)}, u32[]{:S(2)}, u32[]{:S(2)}) collective-permute-start(bf16[256,1024]{0,1:T(8,128)(2,1)} %copy.132), channel_id=1, source_target_pairs={{0,4},{4,8},{8,12},{12,16},{16,20},{20,24},{24,28},{28,32},{32,36}... | collective-permute-start | bytes 1572872 | tf_op jit(solution)/shard_map/while/body/eval_jaxpr/ppermute | solution.py:16
  426.8 4.9 collective-permute-done
  433.6 7.4 %collective-permute-start = (bf16[256,1024]{0,1:T(8,128)(2,1)}, bf16[256,1024]{0,1:T(8,128)(2,1)}, u32[]{:S(2)}, u32[]{:S(2)}) collective-permute-start(bf16[256,1024]{0,1:T(8,128)(2,1)} %copy.132), channel_id=1, source_target_pairs={{0,4},{4,8},{8,12},{12,16},{16,20},{20,24},{24,28},{28,32},{32,36}... | collective-permute-start | bytes 1572872 | tf_op jit(solution)/shard_map/while/body/eval_jaxpr/ppermute | solution.py:16
  442.5 4.9 collective-permute-done
  449.3 7.4 %collective-permute-start = (bf16[256,1024]{0,1:T(8,128)(2,1)}, bf16[256,1024]{0,1:T(8,128)(2,1)}, u32[]{:S(2)}, u32[]{:S(2)}) collective-permute-start(bf16[256,1024]{0,1:T(8,128)(2,1)} %copy.132), channel_id=1, source_target_pairs={{0,4},{4,8},{8,12},{12,16},{16,20},{20,24},{24,28},{28,32},{32,36}... | collective-permute-start | bytes 1572872 | tf_op jit(solution)/shard_map/while/body/eval_jaxpr/ppermute | solution.py:16
  458.2 4.9 collective-permute-done
  465.0 7.4 %collective-permute-start = (bf16[256,1024]{0,1:T(8,128)(2,1)}, bf16[256,1024]{0,1:T(8,128)(2,1)}, u32[]{:S(2)}, u32[]{:S(2)}) collective-permute-start(bf16[256,1024]{0,1:T(8,128)(2,1)} %copy.132), channel_id=1, source_target_pairs={{0,4},{4,8},{8,12},{12,16},{16,20},{20,24},{24,28},{28,32},{32,36}... | collective-permute-start | bytes 1572872 | tf_op jit(solution)/shard_map/while/body/eval_jaxpr/ppermute | solution.py:16
  473.9 4.9 collective-permute-done
  480.6 7.4 %collective-permute-start = (bf16[256,1024]{0,1:T(8,128)(2,1)}, bf16[256,1024]{0,1:T(8,128)(2,1)}, u32[]{:S(2)}, u32[]{:S(2)}) collective-permute-start(bf16[256,1024]{0,1:T(8,128)(2,1)} %copy.132), channel_id=1, source_target_pairs={{0,4},{4,8},{8,12},{12,16},{16,20},{20,24},{24,28},{28,32},{32,36}... | collective-permute-start | bytes 1572872 | tf_op jit(solution)/shard_map/while/body/eval_jaxpr/ppermute | solution.py:16
  489.5 4.9 collective-permute-done
  496.3 7.4 %collective-permute-start = (bf16[256,1024]{0,1:T(8,128)(2,1)}, bf16[256,1024]{0,1:T(8,128)(2,1)}, u32[]{:S(2)}, u32[]{:S(2)}) collective-permute-start(bf16[256,1024]{0,1:T(8,128)(2,1)} %copy.132), channel_id=1, source_target_pairs={{0,4},{4,8},{8,12},{12,16},{16,20},{20,24},{24,28},{28,32},{32,36}... | collective-permute-start | bytes 1572872 | tf_op jit(solution)/shard_map/while/body/eval_jaxpr/ppermute | solution.py:16
  505.2 4.9 collective-permute-done
  514.9 105.6 %all-gather.3.cloned.1.call-done = bf16[1024,2048]{1,0:T(8,128)(2,1)} async-done(((bf16[256,2048]{1,0:T(8,128)(2,1)}), bf16[1024,2048]{1,0:T(8,128)(2,1)}) %all-gather.3.cloned.1.call-update) | async-done | bytes 4194320 | tf_op jit(solution)/shard_map/all_gather | solution.py:133
  (420 shorter events, 269.0 us)
Async XLA Ops:
  7.2 506.0 %copy-start = (bf16[512,2048]{1,0:T(8,128)(2,1)S(1)}, bf16[512,2048]{1,0:T(8,128)(2,1)}, u32[]{:S(2)}) copy-start(bf16[512,2048]{1,0:T(8,128)(2,1)} %param.22) | copy-start | bytes 6291460
  7.2 613.3 %all-gather.3.cloned.1.call-start = ((), (), s32[]{:S(2)}) async-start(), calls=%async_computation | async-start | bytes 5242880 | tf_op jit(solution)/shard_map/all_gather | solution.py:133
  10.4 3.8 copy-start.12
  10.6 3.6 copy-start.1
  10.6 3.6 copy-start.13
  10.6 3.6 copy-start.14
  18.4 9.4 %copy-start.2 = (bf16[256,2048]{1,0:T(8,128)(2,1)S(1)}, bf16[256,2048]{1,0:T(8,128)(2,1)}, u32[]{:S(2)}) copy-start(bf16[256,2048]{1,0:T(8,128)(2,1)} %param.17) | copy-start | bytes 3145732
  19.1 11.8 %copy-start.4 = (bf16[256,2,2,128]{3,0,1,2:T(8,128)(2,1)}, bf16[256,2,2,128]{3,0,1,2:T(8,128)(2,1)S(1)}, u32[]{:S(2)}) copy-start(bf16[256,2,2,128]{3,0,1,2:T(8,128)(2,1)S(1)} %maximum_convert_fusion) | copy-start | bytes 786436
  23.8 18.0 %collective-permute-start.1 = (bf16[256,1024]{1,0:T(8,128)(2,1)}, bf16[256,1024]{1,0:T(8,128)(2,1)}, u32[]{:S(2)}, u32[]{:S(2)}) collective-permute-start(bf16[256,1024]{1,0:T(8,128)(2,1)} %pad_maximum_fusion), channel_id=1, source_target_pairs={{0,4},{4,8},{8,12},{12,16},{16,20},{20,24},{24,28},{28,32},{32,36}... | collective-permute-start | bytes 1572872 | tf_op jit(solution)/shard_map/ppermute | solution.py:16
  32.3 0.9 copy-start.6
  32.3 1.0 copy-start.10
  32.3 1.0 copy-start.11
  32.3 2.0 copy-start.15
  35.9 5.7 copy-start.8
  37.7 3.5 copy-start.7
  45.7 8.3 %collective-permute-start = (bf16[256,1024]{0,1:T(8,128)(2,1)}, bf16[256,1024]{0,1:T(8,128)(2,1)}, u32[]{:S(2)}, u32[]{:S(2)}) collective-permute-start(bf16[256,1024]{0,1:T(8,128)(2,1)} %copy.132), channel_id=1, source_target_pairs={{0,4},{4,8},{8,12},{12,16},{16,20},{20,24},{24,28},{28,32},{32,36}... | collective-permute-start | bytes 1572872 | tf_op jit(solution)/shard_map/while/body/eval_jaxpr/ppermute | solution.py:16
  55.9 10.8 %collective-permute-start = (bf16[256,1024]{0,1:T(8,128)(2,1)}, bf16[256,1024]{0,1:T(8,128)(2,1)}, u32[]{:S(2)}, u32[]{:S(2)}) collective-permute-start(bf16[256,1024]{0,1:T(8,128)(2,1)} %copy.132), channel_id=1, source_target_pairs={{0,4},{4,8},{8,12},{12,16},{16,20},{20,24},{24,28},{28,32},{32,36}... | collective-permute-start | bytes 1572872 | tf_op jit(solution)/shard_map/while/body/eval_jaxpr/ppermute | solution.py:16
  68.6 10.8 %collective-permute-start = (bf16[256,1024]{0,1:T(8,128)(2,1)}, bf16[256,1024]{0,1:T(8,128)(2,1)}, u32[]{:S(2)}, u32[]{:S(2)}) collective-permute-start(bf16[256,1024]{0,1:T(8,128)(2,1)} %copy.132), channel_id=1, source_target_pairs={{0,4},{4,8},{8,12},{12,16},{16,20},{20,24},{24,28},{28,32},{32,36}... | collective-permute-start | bytes 1572872 | tf_op jit(solution)/shard_map/while/body/eval_jaxpr/ppermute | solution.py:16
  81.3 10.8 %collective-permute-start = (bf16[256,1024]{0,1:T(8,128)(2,1)}, bf16[256,1024]{0,1:T(8,128)(2,1)}, u32[]{:S(2)}, u32[]{:S(2)}) collective-permute-start(bf16[256,1024]{0,1:T(8,128)(2,1)} %copy.132), channel_id=1, source_target_pairs={{0,4},{4,8},{8,12},{12,16},{16,20},{20,24},{24,28},{28,32},{32,36}... | collective-permute-start | bytes 1572872 | tf_op jit(solution)/shard_map/while/body/eval_jaxpr/ppermute | solution.py:16
  93.9 12.5 %collective-permute-start = (bf16[256,1024]{0,1:T(8,128)(2,1)}, bf16[256,1024]{0,1:T(8,128)(2,1)}, u32[]{:S(2)}, u32[]{:S(2)}) collective-permute-start(bf16[256,1024]{0,1:T(8,128)(2,1)} %copy.132), channel_id=1, source_target_pairs={{0,4},{4,8},{8,12},{12,16},{16,20},{20,24},{24,28},{28,32},{32,36}... | collective-permute-start | bytes 1572872 | tf_op jit(solution)/shard_map/while/body/eval_jaxpr/ppermute | solution.py:16
  108.3 13.8 %collective-permute-start = (bf16[256,1024]{0,1:T(8,128)(2,1)}, bf16[256,1024]{0,1:T(8,128)(2,1)}, u32[]{:S(2)}, u32[]{:S(2)}) collective-permute-start(bf16[256,1024]{0,1:T(8,128)(2,1)} %copy.132), channel_id=1, source_target_pairs={{0,4},{4,8},{8,12},{12,16},{16,20},{20,24},{24,28},{28,32},{32,36}... | collective-permute-start | bytes 1572872 | tf_op jit(solution)/shard_map/while/body/eval_jaxpr/ppermute | solution.py:16
  124.0 13.8 %collective-permute-start = (bf16[256,1024]{0,1:T(8,128)(2,1)}, bf16[256,1024]{0,1:T(8,128)(2,1)}, u32[]{:S(2)}, u32[]{:S(2)}) collective-permute-start(bf16[256,1024]{0,1:T(8,128)(2,1)} %copy.132), channel_id=1, source_target_pairs={{0,4},{4,8},{8,12},{12,16},{16,20},{20,24},{24,28},{28,32},{32,36}... | collective-permute-start | bytes 1572872 | tf_op jit(solution)/shard_map/while/body/eval_jaxpr/ppermute | solution.py:16
  139.6 13.8 %collective-permute-start = (bf16[256,1024]{0,1:T(8,128)(2,1)}, bf16[256,1024]{0,1:T(8,128)(2,1)}, u32[]{:S(2)}, u32[]{:S(2)}) collective-permute-start(bf16[256,1024]{0,1:T(8,128)(2,1)} %copy.132), channel_id=1, source_target_pairs={{0,4},{4,8},{8,12},{12,16},{16,20},{20,24},{24,28},{28,32},{32,36}... | collective-permute-start | bytes 1572872 | tf_op jit(solution)/shard_map/while/body/eval_jaxpr/ppermute | solution.py:16
  155.3 13.8 %collective-permute-start = (bf16[256,1024]{0,1:T(8,128)(2,1)}, bf16[256,1024]{0,1:T(8,128)(2,1)}, u32[]{:S(2)}, u32[]{:S(2)}) collective-permute-start(bf16[256,1024]{0,1:T(8,128)(2,1)} %copy.132), channel_id=1, source_target_pairs={{0,4},{4,8},{8,12},{12,16},{16,20},{20,24},{24,28},{28,32},{32,36}... | collective-permute-start | bytes 1572872 | tf_op jit(solution)/shard_map/while/body/eval_jaxpr/ppermute | solution.py:16
  171.0 13.8 %collective-permute-start = (bf16[256,1024]{0,1:T(8,128)(2,1)}, bf16[256,1024]{0,1:T(8,128)(2,1)}, u32[]{:S(2)}, u32[]{:S(2)}) collective-permute-start(bf16[256,1024]{0,1:T(8,128)(2,1)} %copy.132), channel_id=1, source_target_pairs={{0,4},{4,8},{8,12},{12,16},{16,20},{20,24},{24,28},{28,32},{32,36}... | collective-permute-start | bytes 1572872 | tf_op jit(solution)/shard_map/while/body/eval_jaxpr/ppermute | solution.py:16
  186.7 13.8 %collective-permute-start = (bf16[256,1024]{0,1:T(8,128)(2,1)}, bf16[256,1024]{0,1:T(8,128)(2,1)}, u32[]{:S(2)}, u32[]{:S(2)}) collective-permute-start(bf16[256,1024]{0,1:T(8,128)(2,1)} %copy.132), channel_id=1, source_target_pairs={{0,4},{4,8},{8,12},{12,16},{16,20},{20,24},{24,28},{28,32},{32,36}... | collective-permute-start | bytes 1572872 | tf_op jit(solution)/shard_map/while/body/eval_jaxpr/ppermute | solution.py:16
  202.4 13.8 %collective-permute-start = (bf16[256,1024]{0,1:T(8,128)(2,1)}, bf16[256,1024]{0,1:T(8,128)(2,1)}, u32[]{:S(2)}, u32[]{:S(2)}) collective-permute-start(bf16[256,1024]{0,1:T(8,128)(2,1)} %copy.132), channel_id=1, source_target_pairs={{0,4},{4,8},{8,12},{12,16},{16,20},{20,24},{24,28},{28,32},{32,36}... | collective-permute-start | bytes 1572872 | tf_op jit(solution)/shard_map/while/body/eval_jaxpr/ppermute | solution.py:16
  218.0 13.8 %collective-permute-start = (bf16[256,1024]{0,1:T(8,128)(2,1)}, bf16[256,1024]{0,1:T(8,128)(2,1)}, u32[]{:S(2)}, u32[]{:S(2)}) collective-permute-start(bf16[256,1024]{0,1:T(8,128)(2,1)} %copy.132), channel_id=1, source_target_pairs={{0,4},{4,8},{8,12},{12,16},{16,20},{20,24},{24,28},{28,32},{32,36}... | collective-permute-start | bytes 1572872 | tf_op jit(solution)/shard_map/while/body/eval_jaxpr/ppermute | solution.py:16
  233.7 13.8 %collective-permute-start = (bf16[256,1024]{0,1:T(8,128)(2,1)}, bf16[256,1024]{0,1:T(8,128)(2,1)}, u32[]{:S(2)}, u32[]{:S(2)}) collective-permute-start(bf16[256,1024]{0,1:T(8,128)(2,1)} %copy.132), channel_id=1, source_target_pairs={{0,4},{4,8},{8,12},{12,16},{16,20},{20,24},{24,28},{28,32},{32,36}... | collective-permute-start | bytes 1572872 | tf_op jit(solution)/shard_map/while/body/eval_jaxpr/ppermute | solution.py:16
  249.4 13.8 %collective-permute-start = (bf16[256,1024]{0,1:T(8,128)(2,1)}, bf16[256,1024]{0,1:T(8,128)(2,1)}, u32[]{:S(2)}, u32[]{:S(2)}) collective-permute-start(bf16[256,1024]{0,1:T(8,128)(2,1)} %copy.132), channel_id=1, source_target_pairs={{0,4},{4,8},{8,12},{12,16},{16,20},{20,24},{24,28},{28,32},{32,36}... | collective-permute-start | bytes 1572872 | tf_op jit(solution)/shard_map/while/body/eval_jaxpr/ppermute | solution.py:16
  265.1 10.8 %collective-permute-start = (bf16[256,1024]{0,1:T(8,128)(2,1)}, bf16[256,1024]{0,1:T(8,128)(2,1)}, u32[]{:S(2)}, u32[]{:S(2)}) collective-permute-start(bf16[256,1024]{0,1:T(8,128)(2,1)} %copy.132), channel_id=1, source_target_pairs={{0,4},{4,8},{8,12},{12,16},{16,20},{20,24},{24,28},{28,32},{32,36}... | collective-permute-start | bytes 1572872 | tf_op jit(solution)/shard_map/while/body/eval_jaxpr/ppermute | solution.py:16
  277.8 12.8 %collective-permute-start = (bf16[256,1024]{0,1:T(8,128)(2,1)}, bf16[256,1024]{0,1:T(8,128)(2,1)}, u32[]{:S(2)}, u32[]{:S(2)}) collective-permute-start(bf16[256,1024]{0,1:T(8,128)(2,1)} %copy.132), channel_id=1, source_target_pairs={{0,4},{4,8},{8,12},{12,16},{16,20},{20,24},{24,28},{28,32},{32,36}... | collective-permute-start | bytes 1572872 | tf_op jit(solution)/shard_map/while/body/eval_jaxpr/ppermute | solution.py:16
  292.4 13.8 %collective-permute-start = (bf16[256,1024]{0,1:T(8,128)(2,1)}, bf16[256,1024]{0,1:T(8,128)(2,1)}, u32[]{:S(2)}, u32[]{:S(2)}) collective-permute-start(bf16[256,1024]{0,1:T(8,128)(2,1)} %copy.132), channel_id=1, source_target_pairs={{0,4},{4,8},{8,12},{12,16},{16,20},{20,24},{24,28},{28,32},{32,36}... | collective-permute-start | bytes 1572872 | tf_op jit(solution)/shard_map/while/body/eval_jaxpr/ppermute | solution.py:16
  308.1 13.8 %collective-permute-start = (bf16[256,1024]{0,1:T(8,128)(2,1)}, bf16[256,1024]{0,1:T(8,128)(2,1)}, u32[]{:S(2)}, u32[]{:S(2)}) collective-permute-start(bf16[256,1024]{0,1:T(8,128)(2,1)} %copy.132), channel_id=1, source_target_pairs={{0,4},{4,8},{8,12},{12,16},{16,20},{20,24},{24,28},{28,32},{32,36}... | collective-permute-start | bytes 1572872 | tf_op jit(solution)/shard_map/while/body/eval_jaxpr/ppermute | solution.py:16
  323.8 13.8 %collective-permute-start = (bf16[256,1024]{0,1:T(8,128)(2,1)}, bf16[256,1024]{0,1:T(8,128)(2,1)}, u32[]{:S(2)}, u32[]{:S(2)}) collective-permute-start(bf16[256,1024]{0,1:T(8,128)(2,1)} %copy.132), channel_id=1, source_target_pairs={{0,4},{4,8},{8,12},{12,16},{16,20},{20,24},{24,28},{28,32},{32,36}... | collective-permute-start | bytes 1572872 | tf_op jit(solution)/shard_map/while/body/eval_jaxpr/ppermute | solution.py:16
  339.5 13.8 %collective-permute-start = (bf16[256,1024]{0,1:T(8,128)(2,1)}, bf16[256,1024]{0,1:T(8,128)(2,1)}, u32[]{:S(2)}, u32[]{:S(2)}) collective-permute-start(bf16[256,1024]{0,1:T(8,128)(2,1)} %copy.132), channel_id=1, source_target_pairs={{0,4},{4,8},{8,12},{12,16},{16,20},{20,24},{24,28},{28,32},{32,36}... | collective-permute-start | bytes 1572872 | tf_op jit(solution)/shard_map/while/body/eval_jaxpr/ppermute | solution.py:16
  355.2 13.8 %collective-permute-start = (bf16[256,1024]{0,1:T(8,128)(2,1)}, bf16[256,1024]{0,1:T(8,128)(2,1)}, u32[]{:S(2)}, u32[]{:S(2)}) collective-permute-start(bf16[256,1024]{0,1:T(8,128)(2,1)} %copy.132), channel_id=1, source_target_pairs={{0,4},{4,8},{8,12},{12,16},{16,20},{20,24},{24,28},{28,32},{32,36}... | collective-permute-start | bytes 1572872 | tf_op jit(solution)/shard_map/while/body/eval_jaxpr/ppermute | solution.py:16
  370.9 13.8 %collective-permute-start = (bf16[256,1024]{0,1:T(8,128)(2,1)}, bf16[256,1024]{0,1:T(8,128)(2,1)}, u32[]{:S(2)}, u32[]{:S(2)}) collective-permute-start(bf16[256,1024]{0,1:T(8,128)(2,1)} %copy.132), channel_id=1, source_target_pairs={{0,4},{4,8},{8,12},{12,16},{16,20},{20,24},{24,28},{28,32},{32,36}... | collective-permute-start | bytes 1572872 | tf_op jit(solution)/shard_map/while/body/eval_jaxpr/ppermute | solution.py:16
  386.5 13.8 %collective-permute-start = (bf16[256,1024]{0,1:T(8,128)(2,1)}, bf16[256,1024]{0,1:T(8,128)(2,1)}, u32[]{:S(2)}, u32[]{:S(2)}) collective-permute-start(bf16[256,1024]{0,1:T(8,128)(2,1)} %copy.132), channel_id=1, source_target_pairs={{0,4},{4,8},{8,12},{12,16},{16,20},{20,24},{24,28},{28,32},{32,36}... | collective-permute-start | bytes 1572872 | tf_op jit(solution)/shard_map/while/body/eval_jaxpr/ppermute | solution.py:16
  402.2 13.8 %collective-permute-start = (bf16[256,1024]{0,1:T(8,128)(2,1)}, bf16[256,1024]{0,1:T(8,128)(2,1)}, u32[]{:S(2)}, u32[]{:S(2)}) collective-permute-start(bf16[256,1024]{0,1:T(8,128)(2,1)} %copy.132), channel_id=1, source_target_pairs={{0,4},{4,8},{8,12},{12,16},{16,20},{20,24},{24,28},{28,32},{32,36}... | collective-permute-start | bytes 1572872 | tf_op jit(solution)/shard_map/while/body/eval_jaxpr/ppermute | solution.py:16
  417.9 13.8 %collective-permute-start = (bf16[256,1024]{0,1:T(8,128)(2,1)}, bf16[256,1024]{0,1:T(8,128)(2,1)}, u32[]{:S(2)}, u32[]{:S(2)}) collective-permute-start(bf16[256,1024]{0,1:T(8,128)(2,1)} %copy.132), channel_id=1, source_target_pairs={{0,4},{4,8},{8,12},{12,16},{16,20},{20,24},{24,28},{28,32},{32,36}... | collective-permute-start | bytes 1572872 | tf_op jit(solution)/shard_map/while/body/eval_jaxpr/ppermute | solution.py:16
  433.6 13.8 %collective-permute-start = (bf16[256,1024]{0,1:T(8,128)(2,1)}, bf16[256,1024]{0,1:T(8,128)(2,1)}, u32[]{:S(2)}, u32[]{:S(2)}) collective-permute-start(bf16[256,1024]{0,1:T(8,128)(2,1)} %copy.132), channel_id=1, source_target_pairs={{0,4},{4,8},{8,12},{12,16},{16,20},{20,24},{24,28},{28,32},{32,36}... | collective-permute-start | bytes 1572872 | tf_op jit(solution)/shard_map/while/body/eval_jaxpr/ppermute | solution.py:16
  449.3 13.8 %collective-permute-start = (bf16[256,1024]{0,1:T(8,128)(2,1)}, bf16[256,1024]{0,1:T(8,128)(2,1)}, u32[]{:S(2)}, u32[]{:S(2)}) collective-permute-start(bf16[256,1024]{0,1:T(8,128)(2,1)} %copy.132), channel_id=1, source_target_pairs={{0,4},{4,8},{8,12},{12,16},{16,20},{20,24},{24,28},{28,32},{32,36}... | collective-permute-start | bytes 1572872 | tf_op jit(solution)/shard_map/while/body/eval_jaxpr/ppermute | solution.py:16
  465.0 13.8 %collective-permute-start = (bf16[256,1024]{0,1:T(8,128)(2,1)}, bf16[256,1024]{0,1:T(8,128)(2,1)}, u32[]{:S(2)}, u32[]{:S(2)}) collective-permute-start(bf16[256,1024]{0,1:T(8,128)(2,1)} %copy.132), channel_id=1, source_target_pairs={{0,4},{4,8},{8,12},{12,16},{16,20},{20,24},{24,28},{28,32},{32,36}... | collective-permute-start | bytes 1572872 | tf_op jit(solution)/shard_map/while/body/eval_jaxpr/ppermute | solution.py:16
  480.6 13.8 %collective-permute-start = (bf16[256,1024]{0,1:T(8,128)(2,1)}, bf16[256,1024]{0,1:T(8,128)(2,1)}, u32[]{:S(2)}, u32[]{:S(2)}) collective-permute-start(bf16[256,1024]{0,1:T(8,128)(2,1)} %copy.132), channel_id=1, source_target_pairs={{0,4},{4,8},{8,12},{12,16},{16,20},{20,24},{24,28},{28,32},{32,36}... | collective-permute-start | bytes 1572872 | tf_op jit(solution)/shard_map/while/body/eval_jaxpr/ppermute | solution.py:16
  496.3 13.8 %collective-permute-start = (bf16[256,1024]{0,1:T(8,128)(2,1)}, bf16[256,1024]{0,1:T(8,128)(2,1)}, u32[]{:S(2)}, u32[]{:S(2)}) collective-permute-start(bf16[256,1024]{0,1:T(8,128)(2,1)} %copy.132), channel_id=1, source_target_pairs={{0,4},{4,8},{8,12},{12,16},{16,20},{20,24},{24,28},{28,32},{32,36}... | collective-permute-start | bytes 1572872 | tf_op jit(solution)/shard_map/while/body/eval_jaxpr/ppermute | solution.py:16
  511.4 1.5 copy-start.9
  620.4 4.3 copy-start.3
  (1 other events, 0.6 us)
Sparse Core Ops, SparseCore 0:
  515.0 105.4 all-gather.2
